TPU v7x, 128 devices: a whole 4x4x4 slice. The times are simulated.
128 devices in a mesh: section: 16 (over y, z_lo, core), sp: 8 (over z_hi, x).
Axes of the slice: x: 4, y: 4, z: 4 (z_hi: 2, z_lo: 2; z = z_hi * 2 + z_lo), core: 2. Of those that a mesh axis runs over, the one named last changes fastest.
Arguments:
- resid: float32 [16, 896, 6144], P('section', 'sp'), may hold values from -1.8 to 1.8
- qkv: bfloat16 [16, 896, 3, 6144], P('section', 'sp'), may hold values from -48 to 48
- cache_kv: bfloat16 [16, 2, 2, 1344, 6144], P('section', None, None, None, 'sp'), may hold values from -6 to 6
- out_proj: bfloat16 [16, 6144, 6144], P('section', 'sp'), may hold values from -0.078125 to 0.078125
- gate: float32 [16, 2, 6144], P('section'), may hold values from 0.5 to 2
- span_ids: int32 [16], P('section'), may hold values from 3 to 39
- cache_counts: int32 [16], P('section'), may hold values from 0 to 3, as said below
- span_mask: int32 [40, 40], replicated, may hold values from 0 to 1, as said below
Outputs:
- carried: float32 [16, 896, 6144], P('section', 'sp')
Inputs may be any that keep to these rules, and one draw needn't show every extreme that they name: `cache_counts`: some section has all 3 slots filled. span_mask[i][j] is 0 for j > i and 1 for j = i.
All inputs are finite; a program needn't handle non-finite values.
Results may differ from a plain program's by a relative error of at most 0.006.
Values may be sent and summed in bfloat16 or wider, within the bound.
No kernel may reach another device: no remote copies, remote signals or barrier semaphores. Data moves between devices by JAX's collectives and lax.ppermute only.
A program may use at most 384 MiB of HBM per device.

v0:
```python
import jax
import jax.numpy as jnp
from jax import lax
from jax.sharding import PartitionSpec as P

HDIM = 128
SPAN = 448
NCHUNK = 40
SLOTS = 3
VIDS = 2
TOKS = 896
KEYS = 1344


def passed_along(shard, axis, by):
    devices = lax.axis_size(axis)
    return lax.ppermute(shard, axis, [(i, (i + by) % devices) for i in range(devices)])


def visible_slots(span_id, filled, span_mask):
    row_mask = lax.dynamic_index_in_dim(span_mask, span_id, 0, keepdims=False)
    slot_ids = jnp.arange(SLOTS, dtype=jnp.int32)
    wanted = span_id - 1 - slot_ids
    columns = jnp.arange(NCHUNK, dtype=jnp.int32)
    looked = jnp.sum(jnp.where(columns[None, :] == wanted[:, None], row_mask[None, :], 0), axis=1)
    return (slot_ids < filled) & (looked == 1)


def far_scores(queries, cache_keys, live_slots):
    score_scale = HDIM ** (-0.5)
    scores = (
        jnp.einsum("qhe,khe->hqk", queries, cache_keys, preferred_element_type=jnp.float32)
        * score_scale
    )
    key_live = jnp.repeat(live_slots, SPAN)
    result = jnp.where(key_live[None, None, :], scores, -jnp.inf)
    return result


def mix_video(far_part, queries, own_keys, own_values, cache_values):
    score_scale = HDIM ** (-0.5)
    near_part = (
        jnp.einsum("qhe,khe->hqk", queries, own_keys, preferred_element_type=jnp.float32)
        * score_scale
    )
    scores = jnp.concatenate([far_part, near_part], axis=2)
    highest = jnp.max(scores, axis=2, keepdims=True)
    raised = jnp.exp(scores - highest)
    weights = (raised / jnp.sum(raised, axis=2, keepdims=True)).astype(jnp.bfloat16)
    values_all = jnp.concatenate([cache_values, own_values], axis=0)
    mixed = jnp.einsum("hqk,khe->qhe", weights, values_all, preferred_element_type=jnp.float32)
    return mixed.astype(jnp.bfloat16).reshape(SPAN, queries.shape[1] * HDIM)


def per_device(resid, qkv, cache_kv, out_proj, gate, span_ids, cache_counts, span_mask):
    own_rows = resid.shape[1]
    local_width = cache_kv.shape[4]
    local_heads = local_width // HDIM
    filled = cache_counts[0]
    live_slots = visible_slots(span_ids[0], filled, span_mask)
    cache_keys = cache_kv[0, 0].reshape(VIDS, KEYS, local_heads, HDIM)
    cache_values = cache_kv[0, 1].reshape(VIDS, KEYS, local_heads, HDIM)

    def score_video(inputs_one):
        return far_scores(inputs_one[0], inputs_one[1], live_slots)

    spread = lax.all_to_all(qkv[0], "sp", split_axis=2, concat_axis=0, tiled=True)
    queries = spread[:, 0].reshape(VIDS, SPAN, local_heads, HDIM)
    far_all = lax.map(score_video, (queries, cache_keys))
    own_keys = spread[:, 1].reshape(VIDS, SPAN, local_heads, HDIM)
    own_values = spread[:, 2].reshape(VIDS, SPAN, local_heads, HDIM)

    def mix_one(inputs_one):
        return mix_video(inputs_one[0], inputs_one[1], inputs_one[2], inputs_one[3], inputs_one[4])

    heads_all = lax.map(mix_one, (far_all, queries, own_keys, own_values, cache_values)).reshape(
        TOKS, local_width
    )
    projected = lax.psum_scatter(
        jnp.dot(heads_all, out_proj[0], preferred_element_type=jnp.float32),
        "sp",
        scatter_dimension=0,
        tiled=True,
    )
    device_place = lax.axis_index("sp")
    video_of = (device_place * own_rows + jnp.arange(own_rows, dtype=jnp.int32)) // SPAN
    picker = (video_of[:, None] == jnp.arange(VIDS, dtype=jnp.int32)[None, :]).astype(jnp.float32)
    gains = jnp.dot(picker, gate[0], precision=lax.Precision.HIGHEST)
    layer_out = resid[0] + gains * projected
    return passed_along(layer_out[None], "section", 1)


def solution(mesh):
    in_specs = (
        P("section", "sp", None),
        P("section", "sp", None, None),
        P("section", None, None, None, "sp"),
        P("section", "sp", None),
        P("section", None, None),
        P("section"),
        P("section"),
        P(),
    )
    out_specs = P("section", "sp", None)
    return jax.shard_map(
        per_device, mesh=mesh, in_specs=in_specs, out_specs=out_specs, check_vma=False
    )
```

profile of v0, /device:TPU:0, one launch (start us, length us, event | category | flops | bytes accessed | tf_op | source)
XLA Modules:
  0.0 543.8 jit_solution(14017527695531019002)
XLA Ops:
  6.5 0.0 copy-start
  6.5 10.0 %copy.53 = bf16[1,112,3,6144]{1,2,3,0:T(4,128)(2,1)} copy(bf16[1,112,3,6144]{3,1,2,0:T(8,128)(2,1)} %param.13) | data formatting | bytes 8257536 | tf_op args[1]
  16.5 7.7 %all-to-all-start = ((bf16[112,3,6144]{0,1,2:T(4,128)(2,1)}), bf16[112,3,6144]{0,1,2:T(4,128)(2,1)}, u32[]{:S(2)}, u32[]{:S(2)}) async-start(bf16[112,3,6144]{0,1,2:T(4,128)(2,1)} %bitcast.81), calls=%async_computation | async-start | bytes 12582912 | tf_op jit(solution)/shard_map/all_to_all | solution.py:67
  24.3 0.0 reduce-scatter.2.cloned.1.call-start
  25.6 5.7 %fusion.31 = (bf16[1,1,2,1344,768]{4,3,2,1,0:T(8,128)(2,1)}, bf16[1,1,2,1344,768]{4,3,2,1,0:T(8,128)(2,1)}) fusion(bf16[1,2,2,1344,768]{4,3,2,1,0:T(8,128)(2,1)} %param.14), kind=kLoop, calls=%fused_computation.44 | loop fusion | bytes 16515072 | tf_op jit(solution)/shard_map/slice | solution.py:61
  31.3 6.4 %copy.58 = bf16[1,1,2,1344,768]{3,4,2,1,0:T(8,128)(2,1)} copy(bf16[1,1,2,1344,768]{4,3,2,1,0:T(8,128)(2,1)} %get-tuple-element.147) | data formatting | bytes 8257536 | tf_op jit(solution)/shard_map/slice | solution.py:61
  37.8 6.4 %copy.60 = bf16[2,1344,6,128]{3,1,2,0:T(8,128)(2,1)} copy(bf16[2,1344,6,128]{1,3,2,0:T(8,128)(2,1)} %bitcast.82) | data formatting | bytes 8257536 | tf_op jit(solution)/shard_map/while | solution.py:69
  44.2 6.4 %copy.52 = bf16[1,1,2,1344,768]{3,4,2,1,0:T(8,128)(2,1)} copy(bf16[1,1,2,1344,768]{4,3,2,1,0:T(8,128)(2,1)} %get-tuple-element.148) | data formatting | bytes 8257536 | tf_op jit(solution)/shard_map/slice | solution.py:62
  50.6 6.4 %copy.62 = bf16[2,1344,6,128]{3,1,2,0:T(8,128)(2,1)} copy(bf16[2,1344,6,128]{1,3,2,0:T(8,128)(2,1)} %bitcast.83) | data formatting | bytes 8257536 | tf_op jit(solution)/shard_map/while | solution.py:76
  57.1 0.7 dynamic-slice_bitcast_fusion.3
  57.8 0.2 select_reduce_fusion
  57.9 39.8 %all-to-all-done = bf16[112,3,6144]{0,1,2:T(4,128)(2,1)} async-done(((bf16[112,3,6144]{0,1,2:T(4,128)(2,1)}), bf16[112,3,6144]{0,1,2:T(4,128)(2,1)}, u32[]{:S(2)}, u32[]{:S(2)}) %all-to-all-start) | async-done | bytes 4128800 | tf_op jit(solution)/shard_map/all_to_all | solution.py:67
  97.7 10.0 %copy.68 = bf16[112,3,8,768]{3,0,2,1:T(8,128)(2,1)} copy(bf16[112,3,8,768]{0,1,3,2:T(4,128)(2,1)} %bitcast.14) | data formatting | bytes 8257536 | tf_op jit(solution)/shard_map/all_to_all | solution.py:67
  107.8 3.5 fusion.32
  111.3 2.5 reshape.32
  113.8 1.7 copy.59
  115.5 18.3 %while.20 = (s32[]{:T(128)}, f32[2,6,448,1344]{3,2,1,0:T(8,128)}, pred[3]{0:T(512)(128)(4,1)S(1)}, bf16[2,448,6,128]{3,1,2,0:T(8,128)(2,1)S(1)}, bf16[2,1344,6,128]{3,1,2,0:T(8,128)(2,1)}, /*index=5*/s32[]{:T(128)}) while((s32[]{:T(128)}, f32[2,6,448,1344]{3,2,1,0:T(8,128)}, pred[3]{0:T(512)(128)(4,1)S(1)}, ...), condition=%wide.region_2.3_spmd, body=%wide.region_1.2_spmd.sunk | while | flops 932069376 | bytes 17899016 | solution.py:69
  115.5 0.1 broadcast_in_dim.71
  115.6 0.1 broadcast_in_dim.72
  115.6 9.0 %bitcast_dynamic-update-slice_fusion.2 = f32[2,6,448,1344]{3,2,1,0:T(8,128)} fusion(f32[2,6,448,1344]{3,2,1,0:T(8,128)} %get-tuple-element.241, s32[]{:T(128)} %get-tuple-element.240, pred[1344]{0:T(1024)(128)(4,1)S(1)} %broadcast_in_dim.72, bf16[2,1344,6,128]{3,1,2,0:T(8,128)(2,1)} %get-tuple-element.250, ...), kind=kOutput, calls=%fused_computation.clone.1 | convolution fusion | flops 932069376 | bytes 17894912 | tf_op jit(solution)/shard_map/while/body/eval_jaxpr/qhe,khe->hqk/dot_general | solution.py:32
  124.6 0.1 broadcast_in_dim.71
  124.7 0.1 broadcast_in_dim.72
  124.8 9.0 %bitcast_dynamic-update-slice_fusion.2 = f32[2,6,448,1344]{3,2,1,0:T(8,128)} fusion(f32[2,6,448,1344]{3,2,1,0:T(8,128)} %get-tuple-element.241, s32[]{:T(128)} %get-tuple-element.240, pred[1344]{0:T(1024)(128)(4,1)S(1)} %broadcast_in_dim.72, bf16[2,1344,6,128]{3,1,2,0:T(8,128)(2,1)} %get-tuple-element.250, ...), kind=kOutput, calls=%fused_computation.clone.1 | convolution fusion | flops 932069376 | bytes 17894912 | tf_op jit(solution)/shard_map/while/body/eval_jaxpr/qhe,khe->hqk/dot_general | solution.py:32
  133.8 4.1 reshape.30
  138.0 2.8 copy.63
  140.8 2.5 reshape.31
  143.2 2.8 copy.65
  146.0 81.0 %while.21 = (s32[]{:T(128)}, bf16[2,448,768]{2,1,0:T(8,128)(2,1)}, bf16[2,1344,6,128]{3,1,2,0:T(8,128)(2,1)}, bf16[2,448,6,128]{3,1,2,0:T(8,128)(2,1)}, f32[2,6,...) while((s32[]{:T(128)}, bf16[2,448,768]{2,1,0:T(8,128)(2,1)}, ...), condition=%wide.region_7.8_spmd, body=%wide.region_3.7_spmd.sunk | while | flops 1586989824 | bytes 108822680 | solution.py:76
  146.0 4.4 fusion.43
  150.4 11.6 %dynamic-slice_reduce_fusion.2 = (f32[6,448]{1,0:T(8,128)S(1)}, f32[6,448,1344]{2,1,0:T(8,128)}) fusion(f32[2,6,448,1344]{3,2,1,0:T(8,128)} %get-tuple-element.272, s32[]{:T(128)} %get-tuple-element.260), kind=kLoop, calls=%fused_computation.9.clone.1 | loop fusion | flops 3609984 | bytes 28912132 | tf_op jit(solution)/shard_map/while/body/eval_jaxpr/reduce_max | solution.py:47
  162.0 0.0 copy-start.1
  162.0 10.8 %fusion.44 = f32[6,448]{1,0:T(8,128)S(1)} fusion(f32[6,448,448]{2,1,0:T(8,128)} %get-tuple-element.230, f32[6,448,1344]{2,1,0:T(8,128)} %get-tuple-element.231, f32[6,448]{1,0:T(8,128)S(1)} %reduce_max.27), kind=kLoop, calls=%fused_computation.11.clone.1 | loop fusion | flops 14448000 | bytes 19289088 | tf_op jit(solution)/shard_map/while/body/eval_jaxpr/reduce_sum | solution.py:49
  172.8 0.0 copy-start.2
  172.8 0.0 copy-done.1
  172.9 0.1 dynamic-slice_bitcast_fusion.7
  173.0 1.2 copy-done.2
  174.2 0.9 dynamic-slice_bitcast_fusion.6
  175.1 10.0 %fusion.45 = bf16[448,6,128]{2,0,1:T(8,128)(2,1)S(1)} fusion(bf16[448,6,128]{2,0,1:T(8,128)(2,1)} %dynamic-slice_bitcast_fusion.6, bf16[1344,6,128]{2,0,1:T(8,128)(2,1)S(1)} %dynamic-slice_bitcast_fusion.7, f32[6,448,448]{2,1,0:T(8,128)} %get-tuple-element.230, f32[6,448,1344]{2,1,0:T(8,128)} %get-tuple-element.231, f32[6,448]{1,0:T(8,128)S(1)} %fusion.44, ...), kind=kOutput, calls=%fused_computation.19.clone.1 | convolution fusion | flops 1258242048 | bytes 22729728 | tf_op jit(solution)/shard_map/while/body/eval_jaxpr/hqk,khe->qhe/dot_general | solution.py:51
  185.1 0.3 copy.79
  185.4 0.3 copy.80
  185.7 0.9 constant_dynamic-update-slice_fusion.2
  186.6 4.4 fusion.43
  190.9 11.6 %dynamic-slice_reduce_fusion.2 = (f32[6,448]{1,0:T(8,128)S(1)}, f32[6,448,1344]{2,1,0:T(8,128)}) fusion(f32[2,6,448,1344]{3,2,1,0:T(8,128)} %get-tuple-element.272, s32[]{:T(128)} %get-tuple-element.260), kind=kLoop, calls=%fused_computation.9.clone.1 | loop fusion | flops 3609984 | bytes 28912132 | tf_op jit(solution)/shard_map/while/body/eval_jaxpr/reduce_max | solution.py:47
  202.5 0.0 copy-start.1
  202.6 10.8 %fusion.44 = f32[6,448]{1,0:T(8,128)S(1)} fusion(f32[6,448,448]{2,1,0:T(8,128)} %get-tuple-element.230, f32[6,448,1344]{2,1,0:T(8,128)} %get-tuple-element.231, f32[6,448]{1,0:T(8,128)S(1)} %reduce_max.27), kind=kLoop, calls=%fused_computation.11.clone.1 | loop fusion | flops 14448000 | bytes 19289088 | tf_op jit(solution)/shard_map/while/body/eval_jaxpr/reduce_sum | solution.py:49
  213.4 0.0 copy-start.2
  213.4 0.0 copy-done.1
  213.4 0.1 dynamic-slice_bitcast_fusion.7
  213.5 1.2 copy-done.2
  214.7 0.9 dynamic-slice_bitcast_fusion.6
  215.6 10.0 %fusion.45 = bf16[448,6,128]{2,0,1:T(8,128)(2,1)S(1)} fusion(bf16[448,6,128]{2,0,1:T(8,128)(2,1)} %dynamic-slice_bitcast_fusion.6, bf16[1344,6,128]{2,0,1:T(8,128)(2,1)S(1)} %dynamic-slice_bitcast_fusion.7, f32[6,448,448]{2,1,0:T(8,128)} %get-tuple-element.230, f32[6,448,1344]{2,1,0:T(8,128)} %get-tuple-element.231, f32[6,448]{1,0:T(8,128)S(1)} %fusion.44, ...), kind=kOutput, calls=%fused_computation.19.clone.1 | convolution fusion | flops 1258242048 | bytes 22729728 | tf_op jit(solution)/shard_map/while/body/eval_jaxpr/hqk,khe->qhe/dot_general | solution.py:51
  225.6 0.3 copy.79
  225.9 0.3 copy.80
  226.2 0.9 constant_dynamic-update-slice_fusion.2
  227.1 16.9 %fusion.24 = f32[896,6144]{1,0:T(8,128)} fusion(bf16[896,768]{1,0:T(8,128)(2,1)} %bitcast.85, bf16[1,768,6144]{2,1,0:T(8,128)(2,1)} %param.15), kind=kOutput, calls=%fused_computation.29 | convolution fusion | flops 8455716864 | bytes 32833536 | tf_op jit(solution)/shard_map/dot_general | solution.py:80
  244.0 0.0 copy-start.3
  244.0 0.0 reduce-scatter.2.cloned.1.call-update
  244.0 253.5 %reduce-scatter.2.cloned.1.call-done = f32[112,6144]{1,0:T(8,128)} async-done(((f32[896,6144]{1,0:T(8,128)}), f32[112,6144]{1,0:T(8,128)}) %reduce-scatter.2.cloned.1.call-update) | async-done | bytes 2752528 | tf_op jit(solution)/shard_map/reduce_scatter | solution.py:79
  497.5 0.0 copy-done
  497.5 0.0 copy-done.3
  497.5 3.3 fusion.27
  500.8 0.1 collective-permute-start
  500.9 34.6 %collective-permute-done = f32[1,112,6144]{2,1,0:T(8,128)S(1)} collective-permute-done((f32[1,112,6144]{2,1,0:T(8,128)S(1)}, f32[1,112,6144]{2,1,0:T(8,128)S(1)}, u32[]{:S(2)}, u32[]{:S(2)}) %collective-permute-start) | collective-permute-done | bytes 2752544 | tf_op jit(solution)/shard_map/ppermute | solution.py:17
  535.4 1.5 copy.100
  (7 shorter events, 0.0 us)
Async XLA Ops:
  6.5 491.0 %copy-start = (f32[1,2,6144]{2,1,0:T(2,128)S(1)}, f32[1,2,6144]{2,1,0:T(2,128)}, u32[]{:S(2)}) copy-start(f32[1,2,6144]{2,1,0:T(2,128)} %param.16) | copy-start | bytes 147460
  16.5 81.2 %all-to-all-start = ((bf16[112,3,6144]{0,1,2:T(4,128)(2,1)}), bf16[112,3,6144]{0,1,2:T(4,128)(2,1)}, u32[]{:S(2)}, u32[]{:S(2)}) async-start(bf16[112,3,6144]{0,1,2:T(4,128)(2,1)} %bitcast.81), calls=%async_computation | async-start | bytes 12582912 | tf_op jit(solution)/shard_map/all_to_all | solution.py:67
  24.3 473.2 %reduce-scatter.2.cloned.1.call-start = ((), (), s32[]{:S(2)}) async-start(), calls=%async_computation.2 | async-start | bytes 24772608 | tf_op jit(solution)/shard_map/reduce_scatter | solution.py:79
  162.0 10.8 %copy-start.1 = (bf16[2,1344,6,128]{3,1,2,0:T(8,128)(2,1)S(1)}, bf16[2,1344,6,128]{3,1,2,0:T(8,128)(2,1)}, u32[]{:S(2)}) copy-start(bf16[2,1344,6,128]{3,1,2,0:T(8,128)(2,1)} %get-tuple-element.270) | copy-start | bytes 12386308 | tf_op jit(solution)/shard_map/while
  172.8 1.3 copy-start.2
  202.5 10.8 %copy-start.1 = (bf16[2,1344,6,128]{3,1,2,0:T(8,128)(2,1)S(1)}, bf16[2,1344,6,128]{3,1,2,0:T(8,128)(2,1)}, u32[]{:S(2)}) copy-start(bf16[2,1344,6,128]{3,1,2,0:T(8,128)(2,1)} %get-tuple-element.270) | copy-start | bytes 12386308 | tf_op jit(solution)/shard_map/while
  213.4 1.3 copy-start.2
  244.0 253.5 %copy-start.3 = (f32[1,112,6144]{2,1,0:T(8,128)S(1)}, f32[1,112,6144]{2,1,0:T(8,128)}, u32[]{:S(2)}) copy-start(f32[1,112,6144]{2,1,0:T(8,128)} %param.12) | copy-start | bytes 8257540
  500.8 34.7 %collective-permute-start = (f32[1,112,6144]{2,1,0:T(8,128)S(1)}, f32[1,112,6144]{2,1,0:T(8,128)S(1)}, u32[]{:S(2)}, u32[]{:S(2)}) collective-permute-start(f32[1,112,6144]{2,1,0:T(8,128)S(1)} %fusion.27), channel_id=1, source_target_pairs={{0,8},{8,16},{16,24},{24,32},{32,40},{40,48},{48,56},{56,64},{64,7... | collective-permute-start | bytes 8257544 | tf_op jit(solution)/shard_map/ppermute | solution.py:17
Sparse Core Ops, SparseCore 0:
  244.1 253.3 reduce-scatter.1
where the time goes:
time: 546 us; the launch traced here: 544 us
  waiting for transfers between devices  328 us (60%)
  local copies, waits for them, and re-layouts  81.2 us (15%)
  matrix products  67 us (12%)
  other arithmetic  45.1 us (8%)
  between operations  14.8 us (3%)
  starting transfers between devices  7.83 us (1%)
    reduce_scatter x1, waiting for transfers between devices, per_device(): lax.psum_scatter(jnp.dot(heads_all, out_proj[0], preferred_element_type=j...  253 us
    all_to_all x1, waiting for transfers between devices, per_device(): lax.all_to_all(qkv[0], 'sp', split_axis=2, concat_axis=0, tiled=True)  39.8 us
    ppermute x1, waiting for transfers between devices, passed_along(): lax.ppermute(shard, axis, [(i, (i + by) % devices) for i in range(devices)])  34.6 us
    reduce_max x4, other arithmetic, mix_video(): highest = jnp.max(scores, axis=2, keepdims=True)  23.2 us
    reduce_sum x2, other arithmetic, mix_video(): jnp.sum(raised, axis=2, keepdims=True)  21.6 us
    dot_general x2, matrix products, mix_video(): jnp.einsum('hqk,khe->qhe', weights, values_all, preferred_element_type=jn...  20.1 us
    dot_general x2, matrix products, far_scores(): jnp.einsum('qhe,khe->hqk', queries, cache_keys, preferred_element_type=jn...  18 us
    dot_general x1, matrix products, per_device(): jnp.dot(heads_all, out_proj[0], preferred_element_type=jnp.float32)  16.9 us
  transfers between devices with their start and end apart: 3, of which 3 were waited for; matrix products, arithmetic and copies ran while one was open for 6% of the time, Pallas kernels for 0%

commit v1 on v0

--- a/solution.py
+++ b/solution.py
@@ -64,7 +64,10 @@
     def score_video(inputs_one):
         return far_scores(inputs_one[0], inputs_one[1], live_slots)
 
-    spread = lax.all_to_all(qkv[0], "sp", split_axis=2, concat_axis=0, tiled=True)
+    spread = jnp.concatenate(
+        lax.all_to_all(jnp.stack(jnp.split(qkv[0], lax.axis_size("sp"), axis=2)), "sp", 0, 0),
+        axis=0,
+    )
     queries = spread[:, 0].reshape(VIDS, SPAN, local_heads, HDIM)
     far_all = lax.map(score_video, (queries, cache_keys))
     own_keys = spread[:, 1].reshape(VIDS, SPAN, local_heads, HDIM)

time: 546 us -> 504 us (0.923)
  waiting for transfers between devices: 328 us -> 296 us
  local copies, waits for them, and re-layouts: 81.2 us -> 72.6 us
    all_to_all x1, waiting for transfers between devices: 39.8 us -> 16.6 us  [per_device(): lax.all_to_all(jnp.stack(jnp.split(qkv[0], lax.axis_size('sp'), axis=2)),...]
    reduce_scatter x1, waiting for transfers between devices: 253 us -> 245 us  [per_device(): lax.psum_scatter(jnp.dot(heads_all, out_proj[0], preferred_element_type=j...]
    all_to_all x1, local copies, waits for them, and re-layouts: 10 us -> 2.52 us  [per_device(): lax.all_to_all(jnp.stack(jnp.split(qkv[0], lax.axis_size('sp'), axis=2)),...]
    unnamed x6 -> x14, local copies, waits for them, and re-layouts: 11.5 us -> 11.8 us
where the time goes in v1:
time: 504 us; the launch traced here: 503 us
  waiting for transfers between devices  296 us (59%)
  local copies, waits for them, and re-layouts  72.6 us (14%)
  matrix products  67 us (13%)
  other arithmetic  45.1 us (9%)
  between operations  14.8 us (3%)
  starting transfers between devices  7.83 us (2%)
    reduce_scatter x1, waiting for transfers between devices, per_device(): lax.psum_scatter(jnp.dot(heads_all, out_proj[0], preferred_element_type=j...  245 us
    ppermute x1, waiting for transfers between devices, passed_along(): lax.ppermute(shard, axis, [(i, (i + by) % devices) for i in range(devices)])  34.6 us
    reduce_max x4, other arithmetic, mix_video(): highest = jnp.max(scores, axis=2, keepdims=True)  23.3 us
    reduce_sum x2, other arithmetic, mix_video(): jnp.sum(raised, axis=2, keepdims=True)  21.6 us
    dot_general x2, matrix products, mix_video(): jnp.einsum('hqk,khe->qhe', weights, values_all, preferred_element_type=jn...  20.1 us
    dot_general x2, matrix products, far_scores(): jnp.einsum('qhe,khe->hqk', queries, cache_keys, preferred_element_type=jn...  18 us
    dot_general x1, matrix products, per_device(): jnp.dot(heads_all, out_proj[0], preferred_element_type=jnp.float32)  16.9 us
    all_to_all x1, waiting for transfers between devices, per_device(): lax.all_to_all(jnp.stack(jnp.split(qkv[0], lax.axis_size('sp'), axis=2)),...  16.6 us
  transfers between devices with their start and end apart: 3, of which 3 were waited for; matrix products, arithmetic and copies ran while one was open for 6% of the time, Pallas kernels for 0%

profile of v1, /device:TPU:0, one launch (start us, length us, event | category | flops | bytes accessed | tf_op | source)
XLA Modules:
  0.0 503.1 jit_solution(15302596802210320885)
XLA Ops:
  6.5 2.0 fusion.35
  8.6 1.8 fusion.34
  10.4 1.9 fusion.33
  12.3 1.9 fusion.32
  14.2 0.0 copy-done.3
  14.2 0.9 fusion.31
  15.0 0.9 fusion.30
  15.9 0.8 fusion.29
  16.8 0.8 fusion.28
  17.6 7.7 %all-to-all-start = ((bf16[8,112,3,768]{3,1,2,0:T(8,128)(2,1)}), bf16[8,112,3,768]{3,1,2,0:T(8,128)(2,1)}, u32[]{:S(2)}, u32[]{:S(2)}) async-start(bf16[8,112,3,768]{3,1,2,0:T(8,128)(2,1)} %fusion.28), calls=%async_computation | async-start | bytes 8257536 | tf_op jit(solution)/shard_map/all_to_all | solution.py:68
  25.3 0.0 reduce-scatter.2.cloned.1.call-start
  26.7 5.7 %fusion.39 = (bf16[1,1,2,1344,768]{4,3,2,1,0:T(8,128)(2,1)}, bf16[1,1,2,1344,768]{4,3,2,1,0:T(8,128)(2,1)}) fusion(bf16[1,2,2,1344,768]{4,3,2,1,0:T(8,128)(2,1)} %param.14), kind=kLoop, calls=%fused_computation.60 | loop fusion | bytes 16515072 | tf_op jit(solution)/shard_map/slice | solution.py:61
  32.3 6.5 %copy.67 = bf16[1,1,2,1344,768]{3,4,2,1,0:T(8,128)(2,1)} copy(bf16[1,1,2,1344,768]{4,3,2,1,0:T(8,128)(2,1)} %get-tuple-element.147) | data formatting | bytes 8257536 | tf_op jit(solution)/shard_map/slice | solution.py:61
  38.8 6.5 %copy.69 = bf16[2,1344,6,128]{3,1,2,0:T(8,128)(2,1)} copy(bf16[2,1344,6,128]{1,3,2,0:T(8,128)(2,1)} %bitcast.109) | data formatting | bytes 8257536 | tf_op jit(solution)/shard_map/while | solution.py:72
  45.2 6.5 %copy.63 = bf16[1,1,2,1344,768]{3,4,2,1,0:T(8,128)(2,1)} copy(bf16[1,1,2,1344,768]{4,3,2,1,0:T(8,128)(2,1)} %get-tuple-element.148) | data formatting | bytes 8257536 | tf_op jit(solution)/shard_map/slice | solution.py:62
  51.7 6.4 %copy.71 = bf16[2,1344,6,128]{3,1,2,0:T(8,128)(2,1)} copy(bf16[2,1344,6,128]{1,3,2,0:T(8,128)(2,1)} %bitcast.110) | data formatting | bytes 8257536 | tf_op jit(solution)/shard_map/while | solution.py:79
  58.1 0.7 dynamic-slice_bitcast_fusion.3
  58.8 0.2 select_reduce_fusion
  59.0 16.6 %all-to-all-done = bf16[8,112,3,768]{3,1,2,0:T(8,128)(2,1)} async-done(((bf16[8,112,3,768]{3,1,2,0:T(8,128)(2,1)}), bf16[8,112,3,768]{3,1,2,0:T(8,128)(2,1)}, u32[]{:S(2)}, u32[]{:S(2)}) %all-to-all-start) | async-done | bytes 4128800 | tf_op jit(solution)/shard_map/all_to_all | solution.py:68
  75.6 2.5 copy.64
  78.1 1.3 fusion.40
  79.5 2.5 reshape.36
  82.0 1.7 copy.68
  83.7 18.3 %while.20 = (s32[]{:T(128)}, f32[2,6,448,1344]{3,2,1,0:T(8,128)}, pred[3]{0:T(512)(128)(4,1)S(1)}, bf16[2,448,6,128]{3,1,2,0:T(8,128)(2,1)S(1)}, bf16[2,1344,6,128]{3,1,2,0:T(8,128)(2,1)}, /*index=5*/s32[]{:T(128)}) while((s32[]{:T(128)}, f32[2,6,448,1344]{3,2,1,0:T(8,128)}, pred[3]{0:T(512)(128)(4,1)S(1)}, ...), condition=%wide.region_2.3_spmd, body=%wide.region_1.2_spmd.sunk | while | flops 932069376 | bytes 17899016 | solution.py:72
  83.7 0.1 broadcast_in_dim.71
  83.7 0.1 broadcast_in_dim.72
  83.8 9.0 %bitcast_dynamic-update-slice_fusion.2 = f32[2,6,448,1344]{3,2,1,0:T(8,128)} fusion(f32[2,6,448,1344]{3,2,1,0:T(8,128)} %get-tuple-element.241, s32[]{:T(128)} %get-tuple-element.240, pred[1344]{0:T(1024)(128)(4,1)S(1)} %broadcast_in_dim.72, bf16[2,1344,6,128]{3,1,2,0:T(8,128)(2,1)} %get-tuple-element.250, ...), kind=kOutput, calls=%fused_computation.clone.1 | convolution fusion | flops 932069376 | bytes 17894912 | tf_op jit(solution)/shard_map/while/body/eval_jaxpr/qhe,khe->hqk/dot_general | solution.py:32
  92.8 0.1 broadcast_in_dim.71
  92.9 0.1 broadcast_in_dim.72
  93.0 9.0 %bitcast_dynamic-update-slice_fusion.2 = f32[2,6,448,1344]{3,2,1,0:T(8,128)} fusion(f32[2,6,448,1344]{3,2,1,0:T(8,128)} %get-tuple-element.241, s32[]{:T(128)} %get-tuple-element.240, pred[1344]{0:T(1024)(128)(4,1)S(1)} %broadcast_in_dim.72, bf16[2,1344,6,128]{3,1,2,0:T(8,128)(2,1)} %get-tuple-element.250, ...), kind=kOutput, calls=%fused_computation.clone.1 | convolution fusion | flops 932069376 | bytes 17894912 | tf_op jit(solution)/shard_map/while/body/eval_jaxpr/qhe,khe->hqk/dot_general | solution.py:32
  102.0 4.1 reshape.34
  106.1 2.8 copy.72
  108.9 2.5 reshape.35
  111.4 2.8 copy.74
  114.2 81.1 %while.21 = (s32[]{:T(128)}, bf16[2,448,768]{2,1,0:T(8,128)(2,1)}, bf16[2,1344,6,128]{3,1,2,0:T(8,128)(2,1)}, bf16[2,448,6,128]{3,1,2,0:T(8,128)(2,1)}, f32[2,6,...) while((s32[]{:T(128)}, bf16[2,448,768]{2,1,0:T(8,128)(2,1)}, ...), condition=%wide.region_7.8_spmd, body=%wide.region_3.7_spmd.sunk | while | flops 1586989824 | bytes 108822680 | solution.py:79
  114.2 4.4 fusion.51
  118.6 11.6 %dynamic-slice_reduce_fusion.2 = (f32[6,448]{1,0:T(8,128)S(1)}, f32[6,448,1344]{2,1,0:T(8,128)}) fusion(f32[2,6,448,1344]{3,2,1,0:T(8,128)} %get-tuple-element.272, s32[]{:T(128)} %get-tuple-element.260), kind=kLoop, calls=%fused_computation.9.clone.1 | loop fusion | flops 3609984 | bytes 28912132 | tf_op jit(solution)/shard_map/while/body/eval_jaxpr/reduce_max | solution.py:47
  130.2 10.8 %fusion.52 = f32[6,448]{1,0:T(8,128)S(1)} fusion(f32[6,448,448]{2,1,0:T(8,128)} %get-tuple-element.230, f32[6,448,1344]{2,1,0:T(8,128)} %get-tuple-element.231, f32[6,448]{1,0:T(8,128)S(1)} %reduce_max.27), kind=kLoop, calls=%fused_computation.11.clone.1 | loop fusion | flops 14448000 | bytes 19289088 | tf_op jit(solution)/shard_map/while/body/eval_jaxpr/reduce_sum | solution.py:49
  141.1 0.1 dynamic-slice_bitcast_fusion.7
  141.2 1.2 copy-done.2
  142.4 0.9 dynamic-slice_bitcast_fusion.6
  143.3 10.0 %fusion.53 = bf16[448,6,128]{2,0,1:T(8,128)(2,1)S(1)} fusion(bf16[448,6,128]{2,0,1:T(8,128)(2,1)} %dynamic-slice_bitcast_fusion.6, bf16[1344,6,128]{2,0,1:T(8,128)(2,1)S(1)} %dynamic-slice_bitcast_fusion.7, f32[6,448,448]{2,1,0:T(8,128)} %get-tuple-element.230, f32[6,448,1344]{2,1,0:T(8,128)} %get-tuple-element.231, f32[6,448]{1,0:T(8,128)S(1)} %fusion.52, ...), kind=kOutput, calls=%fused_computation.19.clone.1 | convolution fusion | flops 1258242048 | bytes 22729728 | tf_op jit(solution)/shard_map/while/body/eval_jaxpr/hqk,khe->qhe/dot_general | solution.py:51
  153.3 0.3 copy.86
  153.6 0.3 copy.87
  153.9 0.9 constant_dynamic-update-slice_fusion.2
  154.8 4.4 fusion.51
  159.1 11.6 %dynamic-slice_reduce_fusion.2 = (f32[6,448]{1,0:T(8,128)S(1)}, f32[6,448,1344]{2,1,0:T(8,128)}) fusion(f32[2,6,448,1344]{3,2,1,0:T(8,128)} %get-tuple-element.272, s32[]{:T(128)} %get-tuple-element.260), kind=kLoop, calls=%fused_computation.9.clone.1 | loop fusion | flops 3609984 | bytes 28912132 | tf_op jit(solution)/shard_map/while/body/eval_jaxpr/reduce_max | solution.py:47
  170.8 10.8 %fusion.52 = f32[6,448]{1,0:T(8,128)S(1)} fusion(f32[6,448,448]{2,1,0:T(8,128)} %get-tuple-element.230, f32[6,448,1344]{2,1,0:T(8,128)} %get-tuple-element.231, f32[6,448]{1,0:T(8,128)S(1)} %reduce_max.27), kind=kLoop, calls=%fused_computation.11.clone.1 | loop fusion | flops 14448000 | bytes 19289088 | tf_op jit(solution)/shard_map/while/body/eval_jaxpr/reduce_sum | solution.py:49
  181.6 0.0 copy-start.2
  181.6 0.0 copy-done.1
  181.6 0.1 dynamic-slice_bitcast_fusion.7
  181.7 1.2 copy-done.2
  182.9 0.9 dynamic-slice_bitcast_fusion.6
  183.8 10.0 %fusion.53 = bf16[448,6,128]{2,0,1:T(8,128)(2,1)S(1)} fusion(bf16[448,6,128]{2,0,1:T(8,128)(2,1)} %dynamic-slice_bitcast_fusion.6, bf16[1344,6,128]{2,0,1:T(8,128)(2,1)S(1)} %dynamic-slice_bitcast_fusion.7, f32[6,448,448]{2,1,0:T(8,128)} %get-tuple-element.230, f32[6,448,1344]{2,1,0:T(8,128)} %get-tuple-element.231, f32[6,448]{1,0:T(8,128)S(1)} %fusion.52, ...), kind=kOutput, calls=%fused_computation.19.clone.1 | convolution fusion | flops 1258242048 | bytes 22729728 | tf_op jit(solution)/shard_map/while/body/eval_jaxpr/hqk,khe->qhe/dot_general | solution.py:51
  193.8 0.3 copy.86
  194.1 0.3 copy.87
  194.4 0.9 constant_dynamic-update-slice_fusion.2
  195.3 16.9 %fusion.24 = f32[896,6144]{1,0:T(8,128)} fusion(bf16[896,768]{1,0:T(8,128)(2,1)} %bitcast.120, bf16[1,768,6144]{2,1,0:T(8,128)(2,1)} %param.15), kind=kOutput, calls=%fused_computation.29 | convolution fusion | flops 8455716864 | bytes 32833536 | tf_op jit(solution)/shard_map/dot_general | solution.py:83
  212.2 0.0 reduce-scatter.2.cloned.1.call-update
  212.2 244.5 %reduce-scatter.2.cloned.1.call-done = f32[112,6144]{1,0:T(8,128)} async-done(((f32[896,6144]{1,0:T(8,128)}), f32[112,6144]{1,0:T(8,128)}) %reduce-scatter.2.cloned.1.call-update) | async-done | bytes 2752528 | tf_op jit(solution)/shard_map/reduce_scatter | solution.py:82
  456.8 3.3 fusion.27
  460.0 0.1 collective-permute-start
  460.1 34.6 %collective-permute-done = f32[1,112,6144]{2,1,0:T(8,128)S(1)} collective-permute-done((f32[1,112,6144]{2,1,0:T(8,128)S(1)}, f32[1,112,6144]{2,1,0:T(8,128)S(1)}, u32[]{:S(2)}, u32[]{:S(2)}) %collective-permute-start) | collective-permute-done | bytes 2752544 | tf_op jit(solution)/shard_map/ppermute | solution.py:17
  494.7 1.5 copy.114
  (16 shorter events, 0.1 us)
Async XLA Ops:
  6.5 450.2 %copy-start = (f32[1,2,6144]{2,1,0:T(2,128)S(1)}, f32[1,2,6144]{2,1,0:T(2,128)}, u32[]{:S(2)}) copy-start(f32[1,2,6144]{2,1,0:T(2,128)} %param.16) | copy-start | bytes 147460
  6.5 7.6 %copy-start.3 = (bf16[1,112,3,6144]{3,1,2,0:T(8,128)(2,1)S(1)}, bf16[1,112,3,6144]{3,1,2,0:T(8,128)(2,1)}, u32[]{:S(2)}) copy-start(bf16[1,112,3,6144]{3,1,2,0:T(8,128)(2,1)} %param.13) | copy-start | bytes 12386308
  17.6 58.0 %all-to-all-start = ((bf16[8,112,3,768]{3,1,2,0:T(8,128)(2,1)}), bf16[8,112,3,768]{3,1,2,0:T(8,128)(2,1)}, u32[]{:S(2)}, u32[]{:S(2)}) async-start(bf16[8,112,3,768]{3,1,2,0:T(8,128)(2,1)} %fusion.28), calls=%async_computation | async-start | bytes 8257536 | tf_op jit(solution)/shard_map/all_to_all | solution.py:68
  25.3 431.5 %reduce-scatter.2.cloned.1.call-start = ((), (), s32[]{:S(2)}) async-start(), calls=%async_computation.2 | async-start | bytes 24772608 | tf_op jit(solution)/shard_map/reduce_scatter | solution.py:82
  130.2 10.8 %copy-start.1 = (bf16[2,1344,6,128]{3,1,2,0:T(8,128)(2,1)S(1)}, bf16[2,1344,6,128]{3,1,2,0:T(8,128)(2,1)}, u32[]{:S(2)}) copy-start(bf16[2,1344,6,128]{3,1,2,0:T(8,128)(2,1)} %get-tuple-element.270) | copy-start | bytes 12386308 | tf_op jit(solution)/shard_map/while
  141.0 1.3 copy-start.2
  170.8 10.8 %copy-start.1 = (bf16[2,1344,6,128]{3,1,2,0:T(8,128)(2,1)S(1)}, bf16[2,1344,6,128]{3,1,2,0:T(8,128)(2,1)}, u32[]{:S(2)}) copy-start(bf16[2,1344,6,128]{3,1,2,0:T(8,128)(2,1)} %get-tuple-element.270) | copy-start | bytes 12386308 | tf_op jit(solution)/shard_map/while
  181.6 1.3 copy-start.2
  212.2 244.6 %copy-start.4 = (f32[1,112,6144]{2,1,0:T(8,128)S(1)}, f32[1,112,6144]{2,1,0:T(8,128)}, u32[]{:S(2)}) copy-start(f32[1,112,6144]{2,1,0:T(8,128)} %param.12) | copy-start | bytes 8257540
  460.0 34.7 %collective-permute-start = (f32[1,112,6144]{2,1,0:T(8,128)S(1)}, f32[1,112,6144]{2,1,0:T(8,128)S(1)}, u32[]{:S(2)}, u32[]{:S(2)}) collective-permute-start(f32[1,112,6144]{2,1,0:T(8,128)S(1)} %fusion.27), channel_id=1, source_target_pairs={{0,8},{8,16},{16,24},{24,32},{32,40},{40,48},{48,56},{56,64},{64,7... | collective-permute-start | bytes 8257544 | tf_op jit(solution)/shard_map/ppermute | solution.py:17
Sparse Core Ops, SparseCore 0:
  212.3 244.3 reduce-scatter.1
